TPU v7x, 256 devices: a whole 4x4x8 slice. The times are simulated.
256 devices in a mesh: seq: 32 (over z, y_lo, core), head: 8 (over x, y_hi).
Axes of the slice: x: 4, y: 4 (y_hi: 2, y_lo: 2; y = y_hi * 2 + y_lo), z: 8, core: 2. Of those that a mesh axis runs over, the one named last changes fastest.
Arguments:
- queries: bfloat16 [32768, 1024], P('seq', 'head'), may hold values from -6 to 6
- keys: bfloat16 [32768, 1024], P('seq', 'head'), may hold values from -6 to 6
- values: bfloat16 [32768, 1024], P('seq', 'head'), may hold values from -6 to 6
- gates: bfloat16 [32768, 1024], P('seq', 'head'), may hold values from -6 to 6
- sessions: int32 [32768], P('seq'), may hold values from 0 to 15, never falling along the last dimension, each value on 1 to 3072 neighbouring positions
- score_bias: float32 [8], P('head'), may hold values from -1 to 1
- grad_out: bfloat16 [32768, 1024], P('seq', 'head'), may hold values from -6 to 6
- w_out: bfloat16 [1024, 1024], P('head'), may hold values from -0.1875 to 0.1875
Outputs:
- grad_queries: float32 [32768, 1024], P('seq', 'head')
- grad_keys: float32 [32768, 1024], P('seq', 'head')
- grad_values: float32 [32768, 1024], P('seq', 'head')
- grad_gates: float32 [32768, 1024], P('seq', 'head')
- grad_w_out: float32 [1024, 1024], P('head', 'seq')
Inputs may be any that keep to these rules, and one draw needn't show every extreme that they name: `sessions`: session numbers never fall from one event to the next; every session number is used, each session has 1 to 3072 events and one has exactly 3072.
All inputs are finite; a program needn't handle non-finite values.
Results may differ from a plain program's by a relative error of at most 0.0042.
Values may be sent and summed in bfloat16 or wider, within the bound.
No kernel may reach another device: no remote copies, remote signals or barrier semaphores. Data moves between devices by JAX's collectives and lax.ppermute only.
A program may use at most 128 MiB of HBM per device.

v0:
```python
import math
import jax
import jax.numpy as jnp
from jax import lax
from jax.sharding import PartitionSpec as P

DH = 128
back_steps = (1, 2, 3)
norm_eps = 1e-05


def shifted(block, axis, distance):
    devices = range(lax.axis_size(axis))
    route = [(i - distance, i) for i in devices if i - distance in devices]
    return lax.ppermute(block, axis, route)


def silu_parts(scores):
    sigma = jax.nn.sigmoid(scores)
    return (scores * sigma, sigma * (1.0 + scores * (1.0 - sigma)))


def per_device(queries, keys, values, gates, sessions, score_bias, grad_out, w_out):
    row_count = queries.shape[0]
    feature_count = queries.shape[1]
    head_count = feature_count // DH
    scale = 1.0 / math.sqrt(DH)
    my_index = lax.axis_index("seq")
    q_heads = queries.reshape(row_count, head_count, DH)
    bias_col = score_bias.reshape(head_count, 1, 1)
    offsets = jnp.arange(row_count, dtype=jnp.int32)
    packed = jnp.stack([keys, values])
    windows = [(packed, sessions)]
    for distance in back_steps:
        windows.append(shifted((packed, sessions), "seq", distance))
    prepared = []
    for distance in range(4):
        key_pack, key_sessions = windows[distance]
        allowed = (sessions[:, None] == key_sessions[None, :]) & (my_index >= distance)
        if distance == 0:
            allowed = allowed & (offsets[None, :] <= offsets[:, None])
        k_heads = key_pack[0].reshape(row_count, head_count, DH)
        v_heads = key_pack[1].reshape(row_count, head_count, DH)
        prepared.append((k_heads, v_heads, allowed))

    def pair_scores(query_heads, k_heads):
        raw = jnp.einsum("ihd,jhd->hij", query_heads, k_heads, preferred_element_type=jnp.float32)
        return raw * scale + bias_col

    attended = jnp.zeros((row_count, head_count, DH), jnp.float32)
    for k_heads, v_heads, allowed in prepared:
        act, deriv = silu_parts(pair_scores(q_heads, k_heads))
        weights = jnp.where(allowed[None], act, 0.0).astype(jnp.bfloat16)
        attended = attended + jnp.einsum(
            "hij,jhd->ihd", weights, v_heads, preferred_element_type=jnp.float32
        )
    centered = attended - jnp.mean(attended, axis=-1, keepdims=True)
    inv_std = lax.rsqrt(jnp.mean(centered * centered, axis=-1, keepdims=True) + norm_eps)
    normed = centered * inv_std
    gate_heads = gates.reshape(row_count, head_count, DH).astype(jnp.float32)
    mixed = (normed * gate_heads).astype(jnp.bfloat16).reshape(row_count, feature_count)
    column_block = lax.all_gather(grad_out, "head", axis=1, tiled=True)
    grad_mixed = lax.dot_general(
        column_block, w_out, (((1,), (1,)), ((), ())), preferred_element_type=jnp.float32
    )
    product = lax.dot_general(
        mixed, column_block, (((0,), (0,)), ((), ())), preferred_element_type=jnp.float32
    )
    weight_rows = product
    grad_mixed, weight_rows = (grad_mixed, weight_rows)
    grad_w_out = lax.psum_scatter(weight_rows, "seq", scatter_dimension=1, tiled=True)
    grad_mixed = grad_mixed.reshape(row_count, head_count, DH)
    grad_gates = (grad_mixed * normed).reshape(row_count, feature_count)
    grad_normed = grad_mixed * gate_heads
    grad_attended = (
        grad_normed
        - jnp.mean(grad_normed, axis=-1, keepdims=True)
        - normed * jnp.mean(grad_normed * normed, axis=-1, keepdims=True)
    ) * inv_std
    grad_attended = grad_attended.astype(jnp.bfloat16)
    grad_queries = jnp.zeros((row_count, head_count, DH), jnp.float32)
    key_terms = []
    for window_index in range(4):
        k_heads, v_heads, allowed = prepared[window_index]
        scores = pair_scores(q_heads, k_heads)
        key_act, key_deriv = silu_parts(scores)
        key_weights = jnp.where(allowed[None], key_act, 0.0).astype(jnp.bfloat16)
        values_term = jnp.einsum(
            "hij,ihd->jhd", key_weights, grad_attended, preferred_element_type=jnp.float32
        )
        grad_weights = jnp.einsum(
            "ihd,jhd->hij", grad_attended, v_heads, preferred_element_type=jnp.float32
        )
        grad_scores = jnp.where(allowed[None], grad_weights * key_deriv * scale, 0.0).astype(
            jnp.bfloat16
        )
        keys_term = jnp.einsum(
            "hij,ihd->jhd", grad_scores, q_heads, preferred_element_type=jnp.float32
        )
        grad_scores, term_pair = (
            grad_scores,
            jnp.stack(
                [
                    keys_term.reshape(row_count, feature_count),
                    values_term.reshape(row_count, feature_count),
                ]
            ),
        )
        key_terms.append(term_pair)
        grad_queries = grad_queries + jnp.einsum(
            "hij,jhd->ihd", grad_scores, k_heads, preferred_element_type=jnp.float32
        )
    summed = key_terms[0]
    for distance in back_steps:
        summed = summed + shifted(key_terms[distance], "seq", -distance)
    return (
        grad_queries.reshape(row_count, feature_count),
        summed[0],
        summed[1],
        grad_gates,
        grad_w_out,
    )


def solution(mesh):
    return jax.shard_map(
        per_device,
        mesh=mesh,
        in_specs=(
            P("seq", "head"),
            P("seq", "head"),
            P("seq", "head"),
            P("seq", "head"),
            P("seq"),
            P("head"),
            P("seq", "head"),
            P("head", None),
        ),
        out_specs=(
            P("seq", "head"),
            P("seq", "head"),
            P("seq", "head"),
            P("seq", "head"),
            P("head", "seq"),
        ),
        check_vma=False,
    )
```

profile of v0, /device:TPU:109, one launch (start us, length us, event | category | flops | bytes accessed | tf_op | source)
XLA Modules:
  0.0 251.1 jit_solution(9258880873134055670)
XLA Ops:
  8.4 4.6 %collective-permute-start.2 = (bf16[2,1024,128]{2,1,0:T(8,128)(2,1)S(1)}, bf16[2,1024,128]{2,1,0:T(8,128)(2,1)S(1)}, u32[]{:S(2)}, u32[]{:S(2)}) collective-permute-start(bf16[2,1024,128]{2,1,0:T(8,128)(2,1)S(1)} %pad_maximum_fusion.3), channel_id=1, source_target_pairs={{0,16},{8,24},{16,32},{24,40},{32,48},{40,56},{48,64},{56,72},{64,... | collective-permute-start | bytes 1572872 | tf_op jit(solution)/shard_map/ppermute | solution.py:15
  13.0 3.5 %collective-permute-start.4 = (bf16[2,1024,128]{2,1,0:T(8,128)(2,1)S(1)}, bf16[2,1024,128]{2,1,0:T(8,128)(2,1)S(1)}, u32[]{:S(2)}, u32[]{:S(2)}) collective-permute-start(bf16[2,1024,128]{2,1,0:T(8,128)(2,1)S(1)} %pad_maximum_fusion.3), channel_id=1, source_target_pairs={{0,24},{8,32},{16,40},{24,48},{32,56},{40,64},{48,72},{56,80},{64,... | collective-permute-start | bytes 1572872 | tf_op jit(solution)/shard_map/ppermute | solution.py:15
  16.5 2.5 %collective-permute-start = (bf16[2,1024,128]{2,1,0:T(8,128)(2,1)S(1)}, bf16[2,1024,128]{2,1,0:T(8,128)(2,1)S(1)}, u32[]{:S(2)}, u32[]{:S(2)}) collective-permute-start(bf16[2,1024,128]{2,1,0:T(8,128)(2,1)S(1)} %pad_maximum_fusion.3), channel_id=1, source_target_pairs={{0,8},{8,16},{16,24},{24,32},{32,40},{40,48},{48,56},{56,64},{64,7... | collective-permute-start | bytes 1572872 | tf_op jit(solution)/shard_map/ppermute | solution.py:15
  19.0 3.0 %collective-permute-start.1 = (s32[1024]{0:T(1024)}, s32[1024]{0:T(1024)S(1)}, u32[]{:S(2)}, u32[]{:S(2)}) collective-permute-start(s32[1024]{0:T(1024)} %param.12), channel_id=1, source_target_pairs={{0,8},{8,16},{16,24},{24,32},{32,40},{40,48},{48,56},{56,64},{64,7... | collective-permute-start | bytes 12296 | tf_op jit(solution)/shard_map/ppermute | solution.py:15
  22.0 2.5 %collective-permute-start.3 = (s32[1024]{0:T(1024)}, s32[1024]{0:T(1024)S(1)}, u32[]{:S(2)}, u32[]{:S(2)}) collective-permute-start(s32[1024]{0:T(1024)} %param.12), channel_id=1, source_target_pairs={{0,16},{8,24},{16,32},{24,40},{32,48},{40,56},{48,64},{56,72},{64,... | collective-permute-start | bytes 12296 | tf_op jit(solution)/shard_map/ppermute | solution.py:15
  28.1 2.9 %collective-permute-start.5 = (s32[1024]{0:T(1024)S(1)}, s32[1024]{0:T(1024)S(1)}, u32[]{:S(2)}, u32[]{:S(2)}) collective-permute-start(s32[1024]{0:T(1024)S(1)} %copy-done.36), channel_id=1, source_target_pairs={{0,24},{8,32},{16,40},{24,48},{32,56},{40,64},{48,72},{56,80},{64,... | collective-permute-start | bytes 12296 | tf_op jit(solution)/shard_map/ppermute | solution.py:15
  31.8 3.5 %collective-permute-done.4 = bf16[2,1024,128]{2,1,0:T(8,128)(2,1)S(1)} collective-permute-done((bf16[2,1024,128]{2,1,0:T(8,128)(2,1)S(1)}, bf16[2,1024,128]{2,1,0:T(8,128)(2,1)S(1)}, u32[]{:S(2)}, u32[]{:S(2)}) %collective-permute-start.4) | collective-permute-done | bytes 524320 | tf_op jit(solution)/shard_map/ppermute | solution.py:15
  35.9 5.8 %collective-permute-done.1 = s32[1024]{0:T(1024)S(1)} collective-permute-done((s32[1024]{0:T(1024)}, s32[1024]{0:T(1024)S(1)}, u32[]{:S(2)}, u32[]{:S(2)}) %collective-permute-start.1) | collective-permute-done | bytes 4128 | tf_op jit(solution)/shard_map/ppermute | solution.py:15
  42.6 10.4 %fusion.26 = (bf16[1024,1024]{1,0:T(8,128)(2,1)S(1)}, bf16[1024,1024]{1,0:T(8,128)(2,1)S(1)}, bf16[1024,1024]{1,0:T(8,128)(2,1)S(1)}, bf16[1024,1024]{1,0:T(8,128)(2,1)S(1)}, f32[1024,1024]{0,1:T(8,128)}) fusion(s32[1024]{0:T(1024)S(1)} %collective-permute-done.1, f32[]{:T(128)} %bitcast.295, pred[]{:T(512)S(6)} %ge.13, s32[1024]{0:T(1024)S(1)} %copy-done.36, ...), kind=kOutput, calls=%fused_computation.35 | convolution fusion | flops 312475648 | bytes 25711620 | tf_op jit(solution)/shard_map/ihd,jhd->hij/dot_general | solution.py:47
  56.7 26.8 %all-gather.2.cloned.1.call-done = bf16[1024,1024]{1,0:T(8,128)(2,1)} async-done(((bf16[1024,128]{1,0:T(8,128)(2,1)}), bf16[1024,1024]{1,0:T(8,128)(2,1)}) %all-gather.2.cloned.1.call-update) | async-done | bytes 2097168 | tf_op jit(solution)/shard_map/all_gather | solution.py:62
  83.5 2.6 %fusion.44 = (f32[1024]{0:T(1024)S(1)}, f32[1024,128]{0,1:T(8,128)S(1)}) fusion(f32[128,1024]{1,0:T(8,128)S(1)} %get-tuple-element.20, f32[1024]{0:T(1024)S(1)} %add_rsqrt_fusion, f32[1024]{0:T(1024)S(1)} %broadcast_multiply_fusion.1, bf16[1024,128]{0,1:T(8,128)(2,1)S(1)} %copy.13, bf16[1024,1024]{1,0:T(8,128)(2,1)} %all-gather.2.cloned.1.call-done, ...), kind=kOutput, calls=%fused_computation.87 | convolution fusion | flops 269220864 | bytes 3682304 | tf_op jit(solution)/shard_map/dot_general | solution.py:63
  94.3 4.4 %fusion.32 = bf16[1024,1024]{1,0:T(8,128)(2,1)S(1)} fusion(f32[1024,1024]{0,1:T(8,128)} %get-tuple-element.18, bf16[1024,128]{0,1:T(8,128)(2,1)S(1)} %get-tuple-element.11, s32[1024]{0:T(1024)S(1)} %collective-permute-done.1, f32[]{:T(128)} %bitcast.293, pred[]{:T(512)S(6)} %ge.13, s32[1024]{0:T(1024)S(1)} %copy-done.36, bf16[2,1024,128]{2,1,0:T(8,128)(2,1)} %copy-done.32), kind=kOutput, calls=%fused_computation.41 | convolution fusion | flops 284164096 | bytes 6824449 | tf_op jit(solution)/shard_map/ihd,jhd->hij/dot_general | solution.py:91
  100.5 3.9 %collective-permute-start.6 = (f32[2,1024,128]{2,1,0:T(8,128)}, f32[2,1024,128]{2,1,0:T(8,128)}, u32[]{:S(2)}, u32[]{:S(2)}) collective-permute-start(f32[2,1024,128]{2,1,0:T(8,128)} %pad_maximum_fusion), channel_id=1, source_target_pairs={{8,0},{16,8},{24,16},{32,24},{40,32},{48,40},{56,48},{64,56},{72,6... | collective-permute-start | bytes 3145736 | tf_op jit(solution)/shard_map/ppermute | solution.py:15
  104.4 3.1 %fusion.21 = bf16[1024,1024]{1,0:T(8,128)(2,1)S(1)} fusion(f32[1024,1024]{0,1:T(8,128)S(1)} %copy-done.17, bf16[1024,128]{0,1:T(8,128)(2,1)S(1)} %get-tuple-element.11, s32[1024]{0:T(1024)S(1)} %collective-permute-done.3, f32[]{:T(128)} %bitcast.297, pred[]{:T(512)S(6)} %ge.14, s32[1024]{0:T(1024)S(1)} %copy-done.36, bf16[2,1024,128]{2,1,0:T(8,128)(2,1)S(1)} %copy-done.29), kind=kOutput, calls=%fused_computation.27 | convolution fusion | flops 284164096 | bytes 6823941 | tf_op jit(solution)/shard_map/ihd,jhd->hij/dot_general | solution.py:91
  109.4 3.2 %collective-permute-start.7 = (f32[2,1024,128]{2,1,0:T(8,128)}, f32[2,1024,128]{2,1,0:T(8,128)}, u32[]{:S(2)}, u32[]{:S(2)}) collective-permute-start(f32[2,1024,128]{2,1,0:T(8,128)} %pad_maximum_fusion.1), channel_id=1, source_target_pairs={{16,0},{24,8},{32,16},{40,24},{48,32},{56,40},{64,48},{72,56},{80,... | collective-permute-start | bytes 3145736 | tf_op jit(solution)/shard_map/ppermute | solution.py:15
  112.6 2.9 %fusion.10 = bf16[1024,1024]{1,0:T(8,128)(2,1)S(1)} fusion(f32[1024,1024]{0,1:T(8,128)S(1)} %copy-done.15, bf16[1024,128]{0,1:T(8,128)(2,1)S(1)} %get-tuple-element.11, s32[1024]{0:T(1024)S(1)} %collective-permute-done.5, f32[]{:T(128)} %bitcast.296, pred[]{:T(512)S(6)} %ge.15, s32[1024]{0:T(1024)S(1)} %copy-done.36, bf16[2,1024,128]{2,1,0:T(8,128)(2,1)S(1)} %copy-done.25), kind=kOutput, calls=%fused_computation.13 | convolution fusion | flops 284164096 | bytes 6823941 | tf_op jit(solution)/shard_map/ihd,jhd->hij/dot_general | solution.py:91
  117.4 2.4 collective-permute-start.8
  119.8 3.5 %select_convert_fusion = bf16[1024,1024]{1,0:T(8,128)(2,1)S(1)} fusion(f32[1024,1024]{1,0:T(8,128)S(1)} %copy-done.13, bf16[1024,128]{0,1:T(8,128)(2,1)S(1)} %get-tuple-element.11, bf16[1024,128]{1,0:T(8,128)(2,1)S(1)} %copy-done.31, f32[]{:T(128)} %bitcast.294, s32[1024]{0:T(1024)S(1)} %copy-done.36, pred[]{:T(512)S(6)} %ge.12), kind=kOutput, calls=%fused_computation.42 | convolution fusion | flops 286261248 | bytes 6819845 | tf_op jit(solution)/shard_map/ihd,jhd->hij/dot_general | solution.py:91
  125.9 2.4 fusion.57
  128.4 2.5 convolution_bitcast_fusion.7
  134.1 5.0 %collective-permute-done.7 = f32[2,1024,128]{2,1,0:T(8,128)} collective-permute-done((f32[2,1024,128]{2,1,0:T(8,128)}, f32[2,1024,128]{2,1,0:T(8,128)}, u32[]{:S(2)}, u32[]{:S(2)}) %collective-permute-start.7) | collective-permute-done | bytes 1048608 | tf_op jit(solution)/shard_map/ppermute | solution.py:15
  139.2 11.9 %collective-permute-done.8 = f32[2,1024,128]{2,1,0:T(8,128)} collective-permute-done((f32[2,1024,128]{2,1,0:T(8,128)}, f32[2,1024,128]{2,1,0:T(8,128)}, u32[]{:S(2)}, u32[]{:S(2)}) %collective-permute-start.8) | collective-permute-done | bytes 1048608 | tf_op jit(solution)/shard_map/ppermute | solution.py:15
  151.1 2.1 fusion.40
  154.2 90.0 %reduce-scatter.2.cloned.1.call-done = f32[128,32]{0,1:T(8,128)} async-done(((f32[128,1024]{0,1:T(8,128)}), f32[128,32]{0,1:T(8,128)}) %reduce-scatter.2.cloned.1.call-update) | async-done | bytes 16400 | tf_op jit(solution)/shard_map/reduce_scatter | solution.py:71
  (115 shorter events, 30.2 us)
Async XLA Ops:
  7.2 19.2 %copy-start = (bf16[1024,128]{1,0:T(8,128)(2,1)S(1)}, bf16[1024,128]{1,0:T(8,128)(2,1)}, u32[]{:S(2)}) copy-start(bf16[1024,128]{1,0:T(8,128)(2,1)} %param.8) | copy-start | bytes 786436
  7.2 20.9 %copy-start.36 = (s32[1024]{0:T(1024)S(1)}, s32[1024]{0:T(1024)}, u32[]{:S(2)}) copy-start(s32[1024]{0:T(1024)} %param.12) | copy-start | bytes 12292
  7.2 76.3 %all-gather.2.cloned.1.call-start = ((), (), s32[]{:S(2)}) async-start(), calls=%async_computation.1 | async-start | bytes 2359296 | tf_op jit(solution)/shard_map/all_gather | solution.py:62
  8.4 19.7 %collective-permute-start.2 = (bf16[2,1024,128]{2,1,0:T(8,128)(2,1)S(1)}, bf16[2,1024,128]{2,1,0:T(8,128)(2,1)S(1)}, u32[]{:S(2)}, u32[]{:S(2)}) collective-permute-start(bf16[2,1024,128]{2,1,0:T(8,128)(2,1)S(1)} %pad_maximum_fusion.3), channel_id=1, source_target_pairs={{0,16},{8,24},{16,32},{24,40},{32,48},{40,56},{48,64},{56,72},{64,... | collective-permute-start | bytes 1572872 | tf_op jit(solution)/shard_map/ppermute | solution.py:15
  13.0 22.2 %collective-permute-start.4 = (bf16[2,1024,128]{2,1,0:T(8,128)(2,1)S(1)}, bf16[2,1024,128]{2,1,0:T(8,128)(2,1)S(1)}, u32[]{:S(2)}, u32[]{:S(2)}) collective-permute-start(bf16[2,1024,128]{2,1,0:T(8,128)(2,1)S(1)} %pad_maximum_fusion.3), channel_id=1, source_target_pairs={{0,24},{8,32},{16,40},{24,48},{32,56},{40,64},{48,72},{56,80},{64,... | collective-permute-start | bytes 1572872 | tf_op jit(solution)/shard_map/ppermute | solution.py:15
  16.5 25.3 %collective-permute-start = (bf16[2,1024,128]{2,1,0:T(8,128)(2,1)S(1)}, bf16[2,1024,128]{2,1,0:T(8,128)(2,1)S(1)}, u32[]{:S(2)}, u32[]{:S(2)}) collective-permute-start(bf16[2,1024,128]{2,1,0:T(8,128)(2,1)S(1)} %pad_maximum_fusion.3), channel_id=1, source_target_pairs={{0,8},{8,16},{16,24},{24,32},{32,40},{40,48},{48,56},{56,64},{64,7... | collective-permute-start | bytes 1572872 | tf_op jit(solution)/shard_map/ppermute | solution.py:15
  19.0 22.7 %collective-permute-start.1 = (s32[1024]{0:T(1024)}, s32[1024]{0:T(1024)S(1)}, u32[]{:S(2)}, u32[]{:S(2)}) collective-permute-start(s32[1024]{0:T(1024)} %param.12), channel_id=1, source_target_pairs={{0,8},{8,16},{16,24},{24,32},{32,40},{40,48},{48,56},{56,64},{64,7... | collective-permute-start | bytes 12296 | tf_op jit(solution)/shard_map/ppermute | solution.py:15
  22.0 19.8 %collective-permute-start.3 = (s32[1024]{0:T(1024)}, s32[1024]{0:T(1024)S(1)}, u32[]{:S(2)}, u32[]{:S(2)}) collective-permute-start(s32[1024]{0:T(1024)} %param.12), channel_id=1, source_target_pairs={{0,16},{8,24},{16,32},{24,40},{32,48},{40,56},{48,64},{56,72},{64,... | collective-permute-start | bytes 12296 | tf_op jit(solution)/shard_map/ppermute | solution.py:15
  24.6 219.6 %reduce-scatter.2.cloned.1.call-start = ((), (), s32[]{:S(2)}) async-start(), calls=%async_computation.2 | async-start | bytes 540672 | tf_op jit(solution)/shard_map/reduce_scatter | solution.py:71
  28.1 14.6 %copy-start.12 = (f32[1024,1024]{1,0:T(8,128)}, f32[1024,1024]{1,0:T(8,128)S(1)}, u32[]{:S(2)}) copy-start(f32[1024,1024]{1,0:T(8,128)S(1)} %fusion.64) | copy-start | bytes 12582916
  28.1 13.7 %copy-start.27 = (bf16[2,1024,128]{2,1,0:T(8,128)(2,1)}, bf16[2,1024,128]{2,1,0:T(8,128)(2,1)S(1)}, u32[]{:S(2)}) copy-start(bf16[2,1024,128]{2,1,0:T(8,128)(2,1)S(1)} %collective-permute-done.2) | copy-start | bytes 1572868
  28.1 13.7 %collective-permute-start.5 = (s32[1024]{0:T(1024)S(1)}, s32[1024]{0:T(1024)S(1)}, u32[]{:S(2)}, u32[]{:S(2)}) collective-permute-start(s32[1024]{0:T(1024)S(1)} %copy-done.36), channel_id=1, source_target_pairs={{0,24},{8,32},{16,40},{24,48},{32,56},{40,64},{48,72},{56,80},{64,... | collective-permute-start | bytes 12296 | tf_op jit(solution)/shard_map/ppermute | solution.py:15
  31.7 21.3 %copy-start.16 = (f32[1024,1024]{0,1:T(8,128)}, f32[1024,1024]{0,1:T(8,128)S(1)}, u32[]{:S(2)}) copy-start(f32[1024,1024]{0,1:T(8,128)S(1)} %fusion.58) | copy-start | bytes 12582916
  35.2 19.5 %copy-start.24 = (bf16[2,1024,128]{2,1,0:T(8,128)(2,1)}, bf16[2,1024,128]{2,1,0:T(8,128)(2,1)S(1)}, u32[]{:S(2)}) copy-start(bf16[2,1024,128]{2,1,0:T(8,128)(2,1)S(1)} %collective-permute-done.4) | copy-start | bytes 1572868
  35.9 17.1 %copy-start.14 = (f32[1024,1024]{0,1:T(8,128)}, f32[1024,1024]{0,1:T(8,128)S(1)}, u32[]{:S(2)}) copy-start(f32[1024,1024]{0,1:T(8,128)S(1)} %fusion.61) | copy-start | bytes 12582916
  42.6 10.4 %copy-start.30 = (bf16[1024,128]{1,0:T(8,128)(2,1)S(1)}, bf16[1024,128]{1,0:T(8,128)(2,1)}, u32[]{:S(2)}) copy-start(bf16[1024,128]{1,0:T(8,128)(2,1)} %param.10) | copy-start | bytes 786436
  42.6 11.3 %copy-start.28 = (bf16[2,1024,128]{2,1,0:T(8,128)(2,1)S(1)}, bf16[2,1024,128]{2,1,0:T(8,128)(2,1)}, u32[]{:S(2)}) copy-start(bf16[2,1024,128]{2,1,0:T(8,128)(2,1)} %copy-done.27) | copy-start | bytes 1572868
  54.8 28.7 %copy-start.35 = (bf16[128,1024]{1,0:T(8,128)(2,1)S(1)}, bf16[128,1024]{1,0:T(8,128)(2,1)}, u32[]{:S(2)}) copy-start(bf16[128,1024]{1,0:T(8,128)(2,1)} %param.15) | copy-start | bytes 786436
  98.6 5.7 %copy-start.17 = (f32[1024,1024]{0,1:T(8,128)S(1)}, f32[1024,1024]{0,1:T(8,128)}, u32[]{:S(2)}) copy-start(f32[1024,1024]{0,1:T(8,128)} %copy-done.16) | copy-start | bytes 12582916
  100.5 33.6 %collective-permute-start.6 = (f32[2,1024,128]{2,1,0:T(8,128)}, f32[2,1024,128]{2,1,0:T(8,128)}, u32[]{:S(2)}, u32[]{:S(2)}) collective-permute-start(f32[2,1024,128]{2,1,0:T(8,128)} %pad_maximum_fusion), channel_id=1, source_target_pairs={{8,0},{16,8},{24,16},{32,24},{40,32},{48,40},{56,48},{64,56},{72,6... | collective-permute-start | bytes 3145736 | tf_op jit(solution)/shard_map/ppermute | solution.py:15
  107.5 8.0 %copy-start.1 = (bf16[1024,1024]{1,0:T(8,128)(2,1)}, bf16[1024,1024]{1,0:T(8,128)(2,1)S(1)}, u32[]{:S(2)}) copy-start(bf16[1024,1024]{1,0:T(8,128)(2,1)S(1)} %fusion.21) | copy-start | bytes 6291460
  109.4 29.8 %collective-permute-start.7 = (f32[2,1024,128]{2,1,0:T(8,128)}, f32[2,1024,128]{2,1,0:T(8,128)}, u32[]{:S(2)}, u32[]{:S(2)}) collective-permute-start(f32[2,1024,128]{2,1,0:T(8,128)} %pad_maximum_fusion.1), channel_id=1, source_target_pairs={{16,0},{24,8},{32,16},{40,24},{48,32},{56,40},{64,48},{72,56},{80,... | collective-permute-start | bytes 3145736 | tf_op jit(solution)/shard_map/ppermute | solution.py:15
  115.5 7.8 %copy-start.2 = (bf16[1024,1024]{1,0:T(8,128)(2,1)}, bf16[1024,1024]{1,0:T(8,128)(2,1)S(1)}, u32[]{:S(2)}) copy-start(bf16[1024,1024]{1,0:T(8,128)(2,1)S(1)} %fusion.10) | copy-start | bytes 6291460
  117.4 33.7 %collective-permute-start.8 = (f32[2,1024,128]{2,1,0:T(8,128)}, f32[2,1024,128]{2,1,0:T(8,128)}, u32[]{:S(2)}, u32[]{:S(2)}) collective-permute-start(f32[2,1024,128]{2,1,0:T(8,128)} %pad_maximum_fusion.2), channel_id=1, source_target_pairs={{24,0},{32,8},{40,16},{48,24},{56,32},{64,40},{72,48},{80,56},{88,... | collective-permute-start | bytes 3145736 | tf_op jit(solution)/shard_map/ppermute | solution.py:15
  (24 other events, 95.5 us)
Sparse Core Ops, SparseCore 0:
  24.7 58.7 all-gather.1
  94.4 149.8 reduce-scatter.1
where the time goes:
time: 251 us
  waiting for transfers between devices  143 us (57%)
  matrix products  52.2 us (21%)
  starting transfers between devices  28.7 us (11%)
  between operations  15.4 us (6%)
  other arithmetic  7.54 us (3%)
  local copies, waits for them, and re-layouts  4.13 us (2%)
    reduce_scatter x1, waiting for transfers between devices, per_device(): lax.psum_scatter(weight_rows, 'seq', scatter_dimension=1, tiled=True)  90 us
    ppermute x9, starting transfers between devices, shifted(): return lax.ppermute(block, axis, route)  28.6 us
    all_gather x1, waiting for transfers between devices, per_device(): column_block = lax.all_gather(grad_out, 'head', axis=1, tiled=True)  26.8 us
    ppermute x9, waiting for transfers between devices, shifted(): return lax.ppermute(block, axis, route)  26.3 us
    dot_general x4, matrix products, per_device(): jnp.einsum('ihd,jhd->hij', grad_attended, v_heads, preferred_element_type...  13.9 us
    dot_general x4, matrix products, pair_scores(): jnp.einsum('ihd,jhd->hij', query_heads, k_heads, preferred_element_type=j...  13.4 us
    dot_general x4, matrix products, per_device(): jnp.einsum('hij,ihd->jhd', key_weights, grad_attended, preferred_element_...  6.23 us
    dot_general x4, matrix products, per_device(): jnp.einsum('hij,jhd->ihd', grad_scores, k_heads, preferred_element_type=j...  6.22 us
  transfers between devices with their start and end apart: 11, of which 6 were waited for; matrix products, arithmetic and copies ran while one was open for 20% of the time, Pallas kernels for 0%

commit v1 on v0

--- a/solution.py
+++ b/solution.py
@@ -59,7 +59,9 @@
     normed = centered * inv_std
     gate_heads = gates.reshape(row_count, head_count, DH).astype(jnp.float32)
     mixed = (normed * gate_heads).astype(jnp.bfloat16).reshape(row_count, feature_count)
-    column_block = lax.all_gather(grad_out, "head", axis=1, tiled=True)
+    column_block = jnp.concatenate(
+        lax.all_to_all(jnp.stack([grad_out] * lax.axis_size("head")), "head", 0, 0), axis=1
+    )
     grad_mixed = lax.dot_general(
         column_block, w_out, (((1,), (1,)), ((), ())), preferred_element_type=jnp.float32
     )

time: 251 us -> 233 us (0.928); the launches traced: 251 us -> 229 us
  waiting for transfers between devices: 143 us -> 105 us
  starting transfers between devices: 28.7 us -> 46.8 us
  local copies, waits for them, and re-layouts: 4.13 us -> 8.45 us
  other arithmetic: 7.54 us -> 3.46 us
    reduce_scatter x1, waiting for transfers between devices: 90 us -> 55.1 us  [per_device(): lax.psum_scatter(weight_rows, 'seq', scatter_dimension=1, tiled=True)]
    all_gather x1 -> x0, waiting for transfers between devices: 26.8 us -> none  [per_device(): column_block = lax.all_gather(grad_out, 'head', axis=1, tiled=True)]
    ppermute x9, waiting for transfers between devices: 26.3 us -> 48 us  [shifted(): return lax.ppermute(block, axis, route)]
    ppermute x9, starting transfers between devices: 28.6 us -> 40.8 us  [shifted(): return lax.ppermute(block, axis, route)]
    all_to_all x0 -> x1, starting transfers between devices: none -> 5.97 us  [per_device(): lax.all_to_all(jnp.stack([grad_out] * lax.axis_size('head')), 'head', 0, 0)]
    another operation x3, other arithmetic: 3.2 us -> 0.21 us  [per_device(): jnp.stack([keys_term.reshape(row_count, feature_count), values_term.resha...]
    unnamed x76 -> x53, local copies, waits for them, and re-layouts: 3.1 us -> 5.85 us
  transfers between devices with their start and end apart: 11 -> 11, of which waited for: 6 -> 5; matrix products, arithmetic and copies ran while one was open for 20% -> 21% of each run, Pallas kernels for 0% -> 0%
where the time goes in v1:
time: 233 us; the launch traced here: 229 us
  waiting for transfers between devices  105 us (45%)
  matrix products  50.4 us (22%)
  starting transfers between devices  46.8 us (20%)
  between operations  15.3 us (7%)
  local copies, waits for them, and re-layouts  8.45 us (4%)
  other arithmetic  3.46 us (1%)
    reduce_scatter x1, waiting for transfers between devices, per_device(): lax.psum_scatter(weight_rows, 'seq', scatter_dimension=1, tiled=True)  55.1 us
    ppermute x9, waiting for transfers between devices, shifted(): return lax.ppermute(block, axis, route)  48 us
    ppermute x9, starting transfers between devices, shifted(): return lax.ppermute(block, axis, route)  40.8 us
    dot_general x4, matrix products, per_device(): jnp.einsum('ihd,jhd->hij', grad_attended, v_heads, preferred_element_type...  16.2 us
    dot_general x4, matrix products, pair_scores(): jnp.einsum('ihd,jhd->hij', query_heads, k_heads, preferred_element_type=j...  12.7 us
    dot_general x4, matrix products, per_device(): jnp.einsum('hij,ihd->jhd', key_weights, grad_attended, preferred_element_...  6.25 us
    all_to_all x1, starting transfers between devices, per_device(): lax.all_to_all(jnp.stack([grad_out] * lax.axis_size('head')), 'head', 0, 0)  5.97 us
    unnamed x53, local copies, waits for them, and re-layouts  5.85 us
  transfers between devices with their start and end apart: 11, of which 5 were waited for; matrix products, arithmetic and copies ran while one was open for 21% of the time, Pallas kernels for 0%

profile of v1, /device:TPU:109, one launch (start us, length us, event | category | flops | bytes accessed | tf_op | source)
XLA Modules:
  0.0 229.3 jit_solution(15148480760653211261)
XLA Ops:
  7.2 1.9 pad_maximum_fusion.3
  9.1 4.6 %collective-permute-start.2 = (bf16[2,1024,128]{2,1,0:T(8,128)(2,1)}, bf16[2,1024,128]{2,1,0:T(8,128)(2,1)S(1)}, u32[]{:S(2)}, u32[]{:S(2)}) collective-permute-start(bf16[2,1024,128]{2,1,0:T(8,128)(2,1)} %pad_maximum_fusion.3), channel_id=1, source_target_pairs={{0,16},{8,24},{16,32},{24,40},{32,48},{40,56},{48,64},{56,72},{64,... | collective-permute-start | bytes 1572872 | tf_op jit(solution)/shard_map/ppermute | solution.py:15
  13.8 4.0 %collective-permute-start.1 = (s32[1024]{0:T(1024)}, s32[1024]{0:T(1024)S(1)}, u32[]{:S(2)}, u32[]{:S(2)}) collective-permute-start(s32[1024]{0:T(1024)} %param.12), channel_id=1, source_target_pairs={{0,8},{8,16},{16,24},{24,32},{32,40},{40,48},{48,56},{56,64},{64,7... | collective-permute-start | bytes 12296 | tf_op jit(solution)/shard_map/ppermute | solution.py:15
  17.8 1.9 collective-permute-start.5
  19.7 2.6 %collective-permute-start.3 = (s32[1024]{0:T(1024)}, s32[1024]{0:T(1024)S(1)}, u32[]{:S(2)}, u32[]{:S(2)}) collective-permute-start(s32[1024]{0:T(1024)} %param.12), channel_id=1, source_target_pairs={{0,16},{8,24},{16,32},{24,40},{32,48},{40,56},{48,64},{56,72},{64,... | collective-permute-start | bytes 12296 | tf_op jit(solution)/shard_map/ppermute | solution.py:15
  22.4 4.4 %collective-permute-start.4 = (bf16[2,1024,128]{2,1,0:T(8,128)(2,1)}, bf16[2,1024,128]{2,1,0:T(8,128)(2,1)}, u32[]{:S(2)}, u32[]{:S(2)}) collective-permute-start(bf16[2,1024,128]{2,1,0:T(8,128)(2,1)} %pad_maximum_fusion.3), channel_id=1, source_target_pairs={{0,24},{8,32},{16,40},{24,48},{32,56},{40,64},{48,72},{56,80},{64,... | collective-permute-start | bytes 1572872 | tf_op jit(solution)/shard_map/ppermute | solution.py:15
  29.4 6.0 %all-to-all-start = ((bf16[8,1024,128]{1,2,0:T(8,128)(2,1)}), bf16[8,1024,128]{1,2,0:T(8,128)(2,1)S(1)}, u32[]{:S(2)}, u32[]{:S(2)}) async-start(bf16[8,1024,128]{1,2,0:T(8,128)(2,1)} %stack.32), calls=%async_computation | async-start | bytes 4194304 | tf_op jit(solution)/shard_map/all_to_all | solution.py:63
  37.9 3.3 %collective-permute-start = (bf16[2,1024,128]{2,1,0:T(8,128)(2,1)}, bf16[2,1024,128]{2,1,0:T(8,128)(2,1)S(1)}, u32[]{:S(2)}, u32[]{:S(2)}) collective-permute-start(bf16[2,1024,128]{2,1,0:T(8,128)(2,1)} %pad_maximum_fusion.3), channel_id=1, source_target_pairs={{0,8},{8,16},{16,24},{24,32},{32,40},{40,48},{48,56},{56,64},{64,7... | collective-permute-start | bytes 1572872 | tf_op jit(solution)/shard_map/ppermute | solution.py:15
  42.0 1.8 fusion.61
  43.8 8.5 %collective-permute-done = bf16[2,1024,128]{2,1,0:T(8,128)(2,1)S(1)} collective-permute-done((bf16[2,1024,128]{2,1,0:T(8,128)(2,1)}, bf16[2,1024,128]{2,1,0:T(8,128)(2,1)S(1)}, u32[]{:S(2)}, u32[]{:S(2)}) %collective-permute-start) | collective-permute-done | bytes 524320 | tf_op jit(solution)/shard_map/ppermute | solution.py:15
  52.4 9.4 %fusion.26 = (bf16[1024,1024]{1,0:T(8,128)(2,1)S(1)}, bf16[1024,1024]{1,0:T(8,128)(2,1)S(1)}, bf16[1024,1024]{1,0:T(8,128)(2,1)S(1)}, bf16[1024,1024]{1,0:T(8,128)(2,1)S(1)}, f32[1024,1024]{0,1:T(8,128)}) fusion(s32[1024]{0:T(1024)S(1)} %collective-permute-done.1, f32[]{:T(128)} %bitcast.298, pred[]{:T(512)S(6)} %ge.13, s32[1024]{0:T(1024)S(1)} %copy-done.23, ...), kind=kOutput, calls=%fused_computation.35 | convolution fusion | flops 312475648 | bytes 25711620 | tf_op jit(solution)/shard_map/ihd,jhd->hij/dot_general | solution.py:47
  63.5 2.0 fusion.59
  66.6 1.8 all-to-all-done
  74.4 1.8 convolution_bitcast_fusion.2
  78.0 5.0 %select_convert_fusion = bf16[1024,1024]{1,0:T(8,128)(2,1)S(1)} fusion(f32[1024,1024]{1,0:T(8,128)} %copy-done.9, bf16[1024,128]{0,1:T(8,128)(2,1)S(1)} %get-tuple-element.16, bf16[1024,128]{1,0:T(8,128)(2,1)} %param.10, f32[]{:T(128)} %bitcast.297, s32[1024]{0:T(1024)S(1)} %copy-done.23, pred[]{:T(512)S(6)} %ge.12), kind=kOutput, calls=%fused_computation.42 | convolution fusion | flops 286261248 | bytes 6819845 | tf_op jit(solution)/shard_map/ihd,jhd->hij/dot_general | solution.py:93
  84.0 4.6 %fusion.21 = bf16[1024,1024]{1,0:T(8,128)(2,1)S(1)} fusion(f32[1024,1024]{0,1:T(8,128)} %copy-done.12, bf16[1024,128]{0,1:T(8,128)(2,1)S(1)} %get-tuple-element.16, s32[1024]{0:T(1024)S(1)} %collective-permute-done.3, f32[]{:T(128)} %bitcast.300, pred[]{:T(512)S(6)} %ge.14, s32[1024]{0:T(1024)S(1)} %copy-done.23, bf16[2,1024,128]{2,1,0:T(8,128)(2,1)} %copy-done.18), kind=kOutput, calls=%fused_computation.27 | convolution fusion | flops 284164096 | bytes 6824449 | tf_op jit(solution)/shard_map/ihd,jhd->hij/dot_general | solution.py:93
  90.7 3.8 %fusion.10 = bf16[1024,1024]{1,0:T(8,128)(2,1)S(1)} fusion(f32[1024,1024]{0,1:T(8,128)S(1)} %copy-done.11, bf16[1024,128]{0,1:T(8,128)(2,1)S(1)} %get-tuple-element.16, s32[1024]{0:T(1024)S(1)} %collective-permute-done.5, f32[]{:T(128)} %bitcast.299, pred[]{:T(512)S(6)} %ge.15, s32[1024]{0:T(1024)S(1)} %copy-done.23, ...), kind=kOutput, calls=%fused_computation.13 | convolution fusion | flops 284164096 | bytes 6824449 | tf_op jit(solution)/shard_map/ihd,jhd->hij/dot_general | solution.py:93
  96.9 2.9 %fusion.32 = bf16[1024,1024]{1,0:T(8,128)(2,1)S(1)} fusion(f32[1024,1024]{0,1:T(8,128)S(1)} %copy-done.24, bf16[1024,128]{0,1:T(8,128)(2,1)S(1)} %get-tuple-element.16, s32[1024]{0:T(1024)S(1)} %collective-permute-done.1, f32[]{:T(128)} %bitcast.296, pred[]{:T(512)S(6)} %ge.13, s32[1024]{0:T(1024)S(1)} %copy-done.23, bf16[2,1024,128]{2,1,0:T(8,128)(2,1)S(1)} %copy-done.22), kind=kOutput, calls=%fused_computation.41 | convolution fusion | flops 284164096 | bytes 6823941 | tf_op jit(solution)/shard_map/ihd,jhd->hij/dot_general | solution.py:93
  100.9 14.3 %collective-permute-start.6 = (f32[2,1024,128]{2,1,0:T(8,128)S(1)}, f32[2,1024,128]{2,1,0:T(8,128)S(1)}, u32[]{:S(2)}, u32[]{:S(2)}) collective-permute-start(f32[2,1024,128]{2,1,0:T(8,128)S(1)} %pad_maximum_fusion), channel_id=1, source_target_pairs={{8,0},{16,8},{24,16},{32,24},{40,32},{48,40},{56,48},{64,56},{72,6... | collective-permute-start | bytes 3145736 | tf_op jit(solution)/shard_map/ppermute | solution.py:15
  115.3 1.9 collective-permute-start.8
  117.3 3.7 %collective-permute-start.7 = (f32[2,1024,128]{2,1,0:T(8,128)S(1)}, f32[2,1024,128]{2,1,0:T(8,128)S(1)}, u32[]{:S(2)}, u32[]{:S(2)}) collective-permute-start(f32[2,1024,128]{2,1,0:T(8,128)S(1)} %pad_maximum_fusion.1), channel_id=1, source_target_pairs={{16,0},{24,8},{32,16},{40,24},{48,32},{56,40},{64,48},{72,56},{80,... | collective-permute-start | bytes 3145736 | tf_op jit(solution)/shard_map/ppermute | solution.py:15
  126.7 14.8 %collective-permute-done.8 = f32[2,1024,128]{2,1,0:T(8,128)S(1)} collective-permute-done((f32[2,1024,128]{2,1,0:T(8,128)S(1)}, f32[2,1024,128]{2,1,0:T(8,128)S(1)}, u32[]{:S(2)}, u32[]{:S(2)}) %collective-permute-start.8) | collective-permute-done | bytes 1048608 | tf_op jit(solution)/shard_map/ppermute | solution.py:15
  141.5 24.6 %collective-permute-done.7 = f32[2,1024,128]{2,1,0:T(8,128)S(1)} collective-permute-done((f32[2,1024,128]{2,1,0:T(8,128)S(1)}, f32[2,1024,128]{2,1,0:T(8,128)S(1)}, u32[]{:S(2)}, u32[]{:S(2)}) %collective-permute-start.7) | collective-permute-done | bytes 1048608 | tf_op jit(solution)/shard_map/ppermute | solution.py:15
  167.3 55.1 %reduce-scatter.2.cloned.1.call-done = f32[128,32]{0,1:T(8,128)} async-done(((f32[128,1024]{0,1:T(8,128)}), f32[128,32]{0,1:T(8,128)}) %reduce-scatter.2.cloned.1.call-update) | async-done | bytes 16400 | tf_op jit(solution)/shard_map/reduce_scatter | solution.py:73
  (92 shorter events, 29.1 us)
Async XLA Ops:
  7.2 30.0 %copy-start = (bf16[1024,128]{1,0:T(8,128)(2,1)S(1)}, bf16[1024,128]{1,0:T(8,128)(2,1)}, u32[]{:S(2)}) copy-start(bf16[1024,128]{1,0:T(8,128)(2,1)} %param.8) | copy-start | bytes 786436
  7.2 30.0 %copy-start.13 = (bf16[1024,128]{1,0:T(8,128)(2,1)S(1)}, bf16[1024,128]{1,0:T(8,128)(2,1)}, u32[]{:S(2)}) copy-start(bf16[1024,128]{1,0:T(8,128)(2,1)} %param.9) | copy-start | bytes 786436
  9.1 28.8 %collective-permute-start.2 = (bf16[2,1024,128]{2,1,0:T(8,128)(2,1)}, bf16[2,1024,128]{2,1,0:T(8,128)(2,1)S(1)}, u32[]{:S(2)}, u32[]{:S(2)}) collective-permute-start(bf16[2,1024,128]{2,1,0:T(8,128)(2,1)} %pad_maximum_fusion.3), channel_id=1, source_target_pairs={{0,16},{8,24},{16,32},{24,40},{32,48},{40,56},{48,64},{56,72},{64,... | collective-permute-start | bytes 1572872 | tf_op jit(solution)/shard_map/ppermute | solution.py:15
  13.8 30.1 %collective-permute-start.1 = (s32[1024]{0:T(1024)}, s32[1024]{0:T(1024)S(1)}, u32[]{:S(2)}, u32[]{:S(2)}) collective-permute-start(s32[1024]{0:T(1024)} %param.12), channel_id=1, source_target_pairs={{0,8},{8,16},{16,24},{24,32},{32,40},{40,48},{48,56},{56,64},{64,7... | collective-permute-start | bytes 12296 | tf_op jit(solution)/shard_map/ppermute | solution.py:15
  17.8 26.0 %collective-permute-start.5 = (s32[1024]{0:T(1024)}, s32[1024]{0:T(1024)S(1)}, u32[]{:S(2)}, u32[]{:S(2)}) collective-permute-start(s32[1024]{0:T(1024)} %param.12), channel_id=1, source_target_pairs={{0,24},{8,32},{16,40},{24,48},{32,56},{40,64},{48,72},{56,80},{64,... | collective-permute-start | bytes 12296 | tf_op jit(solution)/shard_map/ppermute | solution.py:15
  19.7 24.1 %collective-permute-start.3 = (s32[1024]{0:T(1024)}, s32[1024]{0:T(1024)S(1)}, u32[]{:S(2)}, u32[]{:S(2)}) collective-permute-start(s32[1024]{0:T(1024)} %param.12), channel_id=1, source_target_pairs={{0,16},{8,24},{16,32},{24,40},{32,48},{40,56},{48,64},{56,72},{64,... | collective-permute-start | bytes 12296 | tf_op jit(solution)/shard_map/ppermute | solution.py:15
  22.4 19.5 %collective-permute-start.4 = (bf16[2,1024,128]{2,1,0:T(8,128)(2,1)}, bf16[2,1024,128]{2,1,0:T(8,128)(2,1)}, u32[]{:S(2)}, u32[]{:S(2)}) collective-permute-start(bf16[2,1024,128]{2,1,0:T(8,128)(2,1)} %pad_maximum_fusion.3), channel_id=1, source_target_pairs={{0,24},{8,32},{16,40},{24,48},{32,56},{40,64},{48,72},{56,80},{64,... | collective-permute-start | bytes 1572872 | tf_op jit(solution)/shard_map/ppermute | solution.py:15
  29.4 38.9 %all-to-all-start = ((bf16[8,1024,128]{1,2,0:T(8,128)(2,1)}), bf16[8,1024,128]{1,2,0:T(8,128)(2,1)S(1)}, u32[]{:S(2)}, u32[]{:S(2)}) async-start(bf16[8,1024,128]{1,2,0:T(8,128)(2,1)} %stack.32), calls=%async_computation | async-start | bytes 4194304 | tf_op jit(solution)/shard_map/all_to_all | solution.py:63
  35.4 187.0 %reduce-scatter.2.cloned.1.call-start = ((), (), s32[]{:S(2)}) async-start(), calls=%async_computation.2 | async-start | bytes 540672 | tf_op jit(solution)/shard_map/reduce_scatter | solution.py:73
  37.9 14.5 %copy-start.9 = (f32[1024,1024]{1,0:T(8,128)}, f32[1024,1024]{1,0:T(8,128)S(1)}, u32[]{:S(2)}) copy-start(f32[1024,1024]{1,0:T(8,128)S(1)} %fusion.64) | copy-start | bytes 12582916
  37.9 14.5 %copy-start.23 = (s32[1024]{0:T(1024)S(1)}, s32[1024]{0:T(1024)}, u32[]{:S(2)}) copy-start(s32[1024]{0:T(1024)} %param.12) | copy-start | bytes 12292
  37.9 24.8 %copy-start.18 = (bf16[2,1024,128]{2,1,0:T(8,128)(2,1)}, bf16[2,1024,128]{2,1,0:T(8,128)(2,1)S(1)}, u32[]{:S(2)}) copy-start(bf16[2,1024,128]{2,1,0:T(8,128)(2,1)S(1)} %collective-permute-done.2) | copy-start | bytes 1572868
  37.9 14.4 %collective-permute-start = (bf16[2,1024,128]{2,1,0:T(8,128)(2,1)}, bf16[2,1024,128]{2,1,0:T(8,128)(2,1)S(1)}, u32[]{:S(2)}, u32[]{:S(2)}) collective-permute-start(bf16[2,1024,128]{2,1,0:T(8,128)(2,1)} %pad_maximum_fusion.3), channel_id=1, source_target_pairs={{0,8},{8,16},{16,24},{24,32},{32,40},{40,48},{48,56},{56,64},{64,7... | collective-permute-start | bytes 1572872 | tf_op jit(solution)/shard_map/ppermute | solution.py:15
  41.9 19.9 %copy-start.12 = (f32[1024,1024]{0,1:T(8,128)}, f32[1024,1024]{0,1:T(8,128)S(1)}, u32[]{:S(2)}) copy-start(f32[1024,1024]{0,1:T(8,128)S(1)} %fusion.58) | copy-start | bytes 12582916
  43.8 18.0 %copy-start.10 = (f32[1024,1024]{0,1:T(8,128)}, f32[1024,1024]{0,1:T(8,128)S(1)}, u32[]{:S(2)}) copy-start(f32[1024,1024]{0,1:T(8,128)S(1)} %fusion.61) | copy-start | bytes 12582916
  52.4 13.2 %copy-start.21 = (bf16[2,1024,128]{2,1,0:T(8,128)(2,1)}, bf16[2,1024,128]{2,1,0:T(8,128)(2,1)S(1)}, u32[]{:S(2)}) copy-start(bf16[2,1024,128]{2,1,0:T(8,128)(2,1)S(1)} %collective-permute-done) | copy-start | bytes 1572868
  52.4 9.5 %copy-start.20 = (bf16[1024,128]{1,0:T(8,128)(2,1)S(1)}, bf16[1024,128]{1,0:T(8,128)(2,1)}, u32[]{:S(2)}) copy-start(bf16[1024,128]{1,0:T(8,128)(2,1)} %param.10) | copy-start | bytes 786436
  77.9 5.0 %copy-start.14 = (f32[1024,128]{0,1:T(8,128)S(1)}, f32[1024,128]{0,1:T(8,128)}, u32[]{:S(2)}) copy-start(f32[1024,128]{0,1:T(8,128)} %get-tuple-element.15) | copy-start | bytes 1572868
  99.8 15.4 %copy-start.16 = (f32[1,1024,128]{2,1,0:T(8,128)S(1)}, f32[1,1024,128]{2,1,0:T(8,128)}, u32[]{:S(2)}) copy-start(f32[1,1024,128]{2,1,0:T(8,128)} %convolution_bitcast_fusion) | copy-start | bytes 1572868
  99.8 17.4 %copy-start.15 = (f32[1,1024,128]{2,1,0:T(8,128)S(1)}, f32[1,1024,128]{2,1,0:T(8,128)}, u32[]{:S(2)}) copy-start(f32[1,1024,128]{2,1,0:T(8,128)} %convolution_bitcast_fusion.2) | copy-start | bytes 1572868
  100.8 20.2 %copy-start.19 = (bf16[2,1024,128]{2,1,0:T(8,128)(2,1)S(1)}, bf16[2,1024,128]{2,1,0:T(8,128)(2,1)}, u32[]{:S(2)}) copy-start(bf16[2,1024,128]{2,1,0:T(8,128)(2,1)} %copy-done.18) | copy-start | bytes 1572868
  100.9 25.7 %collective-permute-start.6 = (f32[2,1024,128]{2,1,0:T(8,128)S(1)}, f32[2,1024,128]{2,1,0:T(8,128)S(1)}, u32[]{:S(2)}, u32[]{:S(2)}) collective-permute-start(f32[2,1024,128]{2,1,0:T(8,128)S(1)} %pad_maximum_fusion), channel_id=1, source_target_pairs={{8,0},{16,8},{24,16},{32,24},{40,32},{48,40},{56,48},{64,56},{72,6... | collective-permute-start | bytes 3145736 | tf_op jit(solution)/shard_map/ppermute | solution.py:15
  115.3 26.2 %collective-permute-start.8 = (f32[2,1024,128]{2,1,0:T(8,128)S(1)}, f32[2,1024,128]{2,1,0:T(8,128)S(1)}, u32[]{:S(2)}, u32[]{:S(2)}) collective-permute-start(f32[2,1024,128]{2,1,0:T(8,128)S(1)} %pad_maximum_fusion.2), channel_id=1, source_target_pairs={{24,0},{32,8},{40,16},{48,24},{56,32},{64,40},{72,48},{80,56},{88,... | collective-permute-start | bytes 3145736 | tf_op jit(solution)/shard_map/ppermute | solution.py:15
  117.3 48.8 %collective-permute-start.7 = (f32[2,1024,128]{2,1,0:T(8,128)S(1)}, f32[2,1024,128]{2,1,0:T(8,128)S(1)}, u32[]{:S(2)}, u32[]{:S(2)}) collective-permute-start(f32[2,1024,128]{2,1,0:T(8,128)S(1)} %pad_maximum_fusion.1), channel_id=1, source_target_pairs={{16,0},{24,8},{32,16},{40,24},{48,32},{56,40},{64,48},{72,56},{80,... | collective-permute-start | bytes 3145736 | tf_op jit(solution)/shard_map/ppermute | solution.py:15
  (12 other events, 36.2 us)
Sparse Core Ops, SparseCore 0:
  78.1 144.3 reduce-scatter.1
